TPU v7x, 512 devices: a whole 4x8x8 slice. The times are simulated.
512 devices in a mesh: dp: 8 (over z), expert: 64 (over y, x, core).
Axes of the slice: x: 4, y: 8, z: 8, core: 2. Of those that a mesh axis runs over, the one named last changes fastest.
Arguments:
- tokens: bfloat16 [65536, 1024], P(('dp', 'expert')), may hold values from -6 to 6
- expert_ids: int32 [65536, 4], P(('dp', 'expert')), may hold values from 0 to 63, all different within a row; in each aligned block of 128 rows (0 to 127, 128 to 255, ...) at most 16 rows name the same one
- gate_probs: float32 [65536, 4], P(('dp', 'expert')), may hold values from 0.05 to 1
- gate_up: bfloat16 [64, 1024, 768], P('expert', 'dp'), may hold values from -0.1875 to 0.1875
- down_proj: bfloat16 [64, 384, 1024], P('expert', None, 'dp'), may hold values from -0.3125 to 0.3125
- cotangent: bfloat16 [65536, 1024], P(('dp', 'expert')), may hold values from -0.75 to 0.75
Outputs:
- moe_out: bfloat16 [65536, 1024], P(('dp', 'expert'))
- token_grads: bfloat16 [65536, 1024], P(('dp', 'expert'))
- gate_grads: float32 [65536, 4], P(('dp', 'expert'))
- gate_up_grads: float32 [64, 1024, 768], P('expert', 'dp')
- down_grads: float32 [64, 384, 1024], P('expert', None, 'dp')
Inputs may be any that keep to these rules, and one draw needn't show every extreme that they name: `expert_ids`: each row names 4 different experts. Among the rows of one device no expert is named more than 16 times, and in every draw some device names some expert exactly 16 times.
All inputs are finite; a program needn't handle non-finite values.
Results may differ from a plain program's by a relative error of at most 0.012.
Values may be sent and summed in bfloat16 or wider, within the bound.
No kernel may reach another device: no remote copies, remote signals or barrier semaphores. Data moves between devices by JAX's collectives and lax.ppermute only.
A program may use at most 64 MiB of HBM per device.

v0:
```python
import jax
import jax.numpy as jnp
from jax import lax
from jax.sharding import PartitionSpec as P


def forward_rows(rows_in, weight_in, weight_out):
    hidden_width = weight_out.shape[0]
    pre_act = jnp.dot(rows_in, weight_in, preferred_element_type=jnp.float32)
    hidden = (jax.nn.silu(pre_act[:, :hidden_width]) * pre_act[:, hidden_width:]).astype(
        jnp.bfloat16
    )
    expert_out = jnp.dot(hidden, weight_out, preferred_element_type=jnp.float32).astype(
        jnp.bfloat16
    )
    return (expert_out, pre_act, hidden)


def backward_rows(rows_in, grad_rows, pre_act, hidden, weight_in, weight_out):
    hidden_width = weight_out.shape[0]
    contract_last = (((1,), (1,)), ((), ()))
    contract_first = (((0,), (0,)), ((), ()))
    grad_hidden = lax.dot_general(
        grad_rows, weight_out, contract_last, preferred_element_type=jnp.float32
    )
    pre_gate = pre_act[:, :hidden_width]
    sigmoid_value = jax.nn.sigmoid(pre_gate)
    grad_gate = (
        grad_hidden
        * pre_act[:, hidden_width:]
        * sigmoid_value
        * (1.0 + pre_gate * (1.0 - sigmoid_value))
    )
    grad_up = grad_hidden * jax.nn.silu(pre_gate)
    grad_pre = jnp.concatenate([grad_gate, grad_up], axis=1).astype(jnp.bfloat16)
    grad_in = lax.dot_general(
        grad_pre, weight_in, contract_last, preferred_element_type=jnp.float32
    ).astype(jnp.bfloat16)
    weight_in_grad = lax.dot_general(
        rows_in, grad_pre, contract_first, preferred_element_type=jnp.float32
    )
    weight_out_grad = lax.dot_general(
        hidden, grad_rows, contract_first, preferred_element_type=jnp.float32
    )
    return (grad_in, weight_in_grad, weight_out_grad)


def live_slots(recv_counts, capacity):
    within = jnp.arange(capacity, dtype=jnp.int32)[None, :] < recv_counts[:, None]
    return within.reshape(-1)


def expert_forward(rows_in, filled, weight_in, weight_out):
    zero_row = jnp.zeros((), jnp.bfloat16)
    expert_out, pre_act, hidden = forward_rows(rows_in, weight_in, weight_out)
    expert_out = jnp.where(filled[:, None], expert_out, zero_row)
    stored = (rows_in, pre_act, hidden, None)
    return (expert_out, stored)


def expert_backward(grads_in, filled, stored, weight_in, weight_out):
    zero_row = jnp.zeros((), jnp.bfloat16)
    rows_in, pre_act, hidden, unused_plan = stored
    grad_back, in_grad, out_grad = backward_rows(
        rows_in, grads_in, pre_act, hidden, weight_in, weight_out
    )
    grad_back = jnp.where(filled[:, None], grad_back, zero_row)
    return (grad_back, in_grad, out_grad)


def local(tokens, expert_ids, gate_probs, gate_up, down_proj, cotangent):
    token_count, top_count = expert_ids.shape
    expert_count = lax.axis_size("expert")
    capacity = 2 * token_count * top_count // expert_count
    route_count = token_count * top_count
    slot_count = expert_count * capacity
    flat_ids = expert_ids.reshape(route_count)
    onehot = (flat_ids[:, None] == jnp.arange(expert_count, dtype=jnp.int32)[None, :]).astype(
        jnp.int32
    )
    slot_index = jnp.sum((jnp.cumsum(onehot, axis=0) - onehot) * onehot, axis=1)
    position = flat_ids * capacity + slot_index
    counts = jnp.sum(onehot, axis=0)
    slot_range = jnp.arange(slot_count, dtype=jnp.int32)
    matches = position[None, :] == slot_range[:, None]
    route_of_slot = jnp.sum(
        jnp.where(matches, jnp.arange(route_count, dtype=jnp.int32)[None, :], 0), axis=1
    )
    slot_filled = jnp.any(matches, axis=1)
    token_of_slot = route_of_slot // top_count
    zero_row = jnp.zeros((), jnp.bfloat16)
    send_tokens = jnp.where(slot_filled[:, None], tokens[token_of_slot], zero_row)
    slot_probs = jnp.where(slot_filled, gate_probs.reshape(route_count)[route_of_slot], 0.0)
    send_grads = (slot_probs[:, None] * cotangent[token_of_slot].astype(jnp.float32)).astype(
        jnp.bfloat16
    )
    weight_in, weight_out = (
        lax.all_gather(gate_up, "dp", axis=1, tiled=True),
        lax.all_gather(down_proj, "dp", axis=2, tiled=True),
    )
    weight_in = weight_in[0]
    weight_out = weight_out[0]
    rows_in, recv_counts = (
        lax.all_to_all(send_tokens, "expert", split_axis=0, concat_axis=0, tiled=True),
        lax.all_to_all(counts, "expert", split_axis=0, concat_axis=0, tiled=True),
    )
    filled = live_slots(recv_counts, capacity)
    expert_out, stored = expert_forward(rows_in, filled, weight_in, weight_out)
    back_out = lax.all_to_all(expert_out, "expert", split_axis=0, concat_axis=0, tiled=True)
    grads_in = lax.all_to_all(send_grads, "expert", split_axis=0, concat_axis=0, tiled=True)
    grad_back, in_grad, out_grad = expert_backward(grads_in, filled, stored, weight_in, weight_out)
    back_grad = lax.all_to_all(grad_back, "expert", split_axis=0, concat_axis=0, tiled=True)
    sum_in, sum_out = (
        lax.psum_scatter(
            in_grad[None].astype(jnp.bfloat16), "dp", scatter_dimension=1, tiled=True
        ).astype(jnp.float32),
        lax.psum_scatter(
            out_grad[None].astype(jnp.bfloat16), "dp", scatter_dimension=2, tiled=True
        ).astype(jnp.float32),
    )
    out_routes = back_out[position].reshape(token_count, top_count, -1).astype(jnp.float32)
    moe_out = jnp.sum(gate_probs[:, :, None] * out_routes, axis=1).astype(jnp.bfloat16)
    gate_grads = jnp.sum(cotangent.astype(jnp.float32)[:, None, :] * out_routes, axis=2)
    grad_routes = back_grad[position].reshape(token_count, top_count, -1).astype(jnp.float32)
    token_grads = jnp.sum(grad_routes, axis=1).astype(jnp.bfloat16)
    return (moe_out, token_grads, gate_grads, sum_in, sum_out)


def solution(mesh):
    return jax.shard_map(
        local,
        mesh=mesh,
        in_specs=(
            P(("dp", "expert"), None),
            P(("dp", "expert"), None),
            P(("dp", "expert"), None),
            P("expert", "dp", None),
            P("expert", None, "dp"),
            P(("dp", "expert"), None),
        ),
        out_specs=(
            P(("dp", "expert"), None),
            P(("dp", "expert"), None),
            P(("dp", "expert"), None),
            P("expert", "dp", None),
            P("expert", None, "dp"),
        ),
        check_vma=False,
    )
```

profile of v0, /device:TPU:2, one launch (start us, length us, event | category | flops | bytes accessed | tf_op | source)
XLA Modules:
  0.0 300.2 jit_solution(8653985739572995588)
XLA Ops:
  10.6 10.7 %all-to-all-start = ((s32[64,1,1]{2,1,0:T(1,128)}), s32[64,1,1]{2,1,0:T(1,128)S(1)}, u32[]{:S(2)}, u32[]{:S(2)}) async-start(s32[64,1,1]{2,1,0:T(1,128)} %copy.36), calls=%async_computation | async-start | bytes 65536 | tf_op jit(solution)/shard_map/all_to_all | solution.py:105
  22.0 4.1 %gather_fusion = bf16[1024,1024]{1,0:T(8,128)(2,1)S(1)} fusion(bf16[128,1024]{1,0:T(8,128)(2,1)S(1)} %copy-done, s32[1024]{0:T(1024)S(1)} %broadcast_clamp_fusion.1), kind=kCustom, calls=%fused_computation | custom fusion | bytes 4198400 | tf_op jit(solution)/shard_map/gather | solution.py:92
  29.8 8.5 %all-to-all-start.1 = ((bf16[64,16,1024]{2,1,0:T(8,128)(2,1)}), bf16[64,16,1024]{2,1,0:T(8,128)(2,1)}, u32[]{:S(2)}, u32[]{:S(2)}) async-start(bf16[64,16,1024]{2,1,0:T(8,128)(2,1)} %broadcast_select_fusion), calls=%async_computation.1 | async-start | bytes 4194304 | tf_op jit(solution)/shard_map/all_to_all | solution.py:104
  38.5 6.9 %gather_fusion.2 = f32[1024]{0:T(1024)S(1)} fusion(f32[512]{0:T(512)S(1)} %reshape.204, s32[1024]{0:T(1024)S(1)} %broadcast_clamp_fusion), kind=kCustom, calls=%fused_computation.2 | custom fusion | bytes 12288 | tf_op jit(solution)/shard_map/gather | solution.py:93
  45.5 4.1 %gather_fusion.3 = bf16[1024,1024]{1,0:T(8,128)(2,1)S(1)} fusion(bf16[128,1024]{1,0:T(8,128)(2,1)S(1)} %copy-done.1, s32[1024]{0:T(1024)S(1)} %broadcast_clamp_fusion.1), kind=kCustom, calls=%fused_computation.3 | custom fusion | bytes 4198400 | tf_op jit(solution)/shard_map/gather | solution.py:94
  51.4 38.1 %all-to-all-done.1 = bf16[64,16,1024]{2,1,0:T(8,128)(2,1)} async-done(((bf16[64,16,1024]{2,1,0:T(8,128)(2,1)}), bf16[64,16,1024]{2,1,0:T(8,128)(2,1)}, u32[]{:S(2)}, u32[]{:S(2)}) %all-to-all-start.1) | async-done | bytes 2097184 | tf_op jit(solution)/shard_map/all_to_all | solution.py:104
  89.4 5.4 %all-to-all-start.3 = ((bf16[64,16,1024]{2,1,0:T(8,128)(2,1)}), bf16[64,16,1024]{2,1,0:T(8,128)(2,1)S(1)}, u32[]{:S(2)}, u32[]{:S(2)}) async-start(bf16[64,16,1024]{2,1,0:T(8,128)(2,1)} %fusion), calls=%async_computation.3 | async-start | bytes 4194304 | tf_op jit(solution)/shard_map/all_to_all | solution.py:110
  95.6 34.6 %all_gather.7 = bf16[1,384,1024]{2,1,0:T(8,128)(2,1)S(1)} all-gather(bf16[1,384,128]{2,1,0:T(8,128)(2,1)} %param.10), channel_id=1, replica_groups=mesh['dp'=8,'expert'=64] {'dp'}, dimensions={2}, use_global_device_ids=true | all-gather | bytes 884736 | tf_op jit(solution)/shard_map/all_gather | solution.py:99
  131.6 15.3 %all-gather.2.cloned.1.call-done = bf16[1,1024,768]{2,1,0:T(8,128)(2,1)} async-done(((bf16[1,128,768]{2,1,0:T(8,128)(2,1)}), bf16[1,1024,768]{2,1,0:T(8,128)(2,1)}) %all-gather.2.cloned.1.call-update) | async-done | bytes 1572880 | tf_op jit(solution)/shard_map/all_gather | solution.py:98
  146.9 5.5 %fusion.3 = f32[1024,768]{0,1:T(8,128)} fusion(bf16[1024,1024]{1,0:T(8,128)(2,1)} %bitcast.5, bf16[1,1024,768]{2,1,0:T(8,128)(2,1)} %all-gather.2.cloned.1.call-done), kind=kOutput, calls=%fused_computation.18 | convolution fusion | flops 1610612736 | bytes 6815744 | tf_op jit(solution)/shard_map/dot_general | solution.py:9
  152.5 5.1 %multiply_convert_fusion.1 = (bf16[1024,384]{0,1:T(8,128)(2,1)S(1)}, bf16[1024,384]{0,1:T(8,128)(2,1)S(1)}, bf16[1024,384]{0,1:T(8,128)(2,1)}) fusion(f32[1024,768]{0,1:T(8,128)} %fusion.3, bf16[1024,1024]{1,0:T(8,128)(2,1)S(1)} %bitcast.60, bf16[1,384,1024]{2,1,0:T(8,128)(2,1)S(1)} %all_gather.7), kind=kOutput, calls=%fused_computation.21 | convolution fusion | flops 811204608 | bytes 8388608 | tf_op jit(solution)/shard_map/dot_general | solution.py:23
  157.6 3.3 %convert_select_fusion = bf16[1024,1024]{1,0:T(8,128)(2,1)} fusion(pred[1024]{0:T(1024)(128)(4,1)S(1)} %lt.50, bf16[1,1024,768]{2,1,0:T(8,128)(2,1)S(1)} %copy-done.6, bf16[1024,384]{0,1:T(8,128)(2,1)S(1)} %get-tuple-element.25, bf16[1024,384]{0,1:T(8,128)(2,1)S(1)} %get-tuple-element.24), kind=kOutput, calls=%fused_computation.8 | convolution fusion | flops 1615855616 | bytes 5243904 | tf_op jit(solution)/shard_map/dot_general | solution.py:36
  160.9 10.3 %all-to-all-start.4 = ((bf16[64,16,1024]{2,1,0:T(8,128)(2,1)}), bf16[64,16,1024]{2,1,0:T(8,128)(2,1)S(1)}, u32[]{:S(2)}, u32[]{:S(2)}) async-start(bf16[64,16,1024]{2,1,0:T(8,128)(2,1)} %bitcast.62), calls=%async_computation.4 | async-start | bytes 4194304 | tf_op jit(solution)/shard_map/all_to_all | solution.py:112
  171.2 3.7 %fusion.7 = bf16[1,384,1024]{2,1,0:T(8,128)(2,1)} fusion(bf16[1024,384]{0,1:T(8,128)(2,1)} %get-tuple-element.26, bf16[1024,1024]{1,0:T(8,128)(2,1)} %bitcast.61), kind=kOutput, calls=%fused_computation.27 | convolution fusion | flops 805699584 | bytes 3670016 | tf_op jit(solution)/shard_map/dot_general | solution.py:42
  174.9 4.8 %copy.42 = bf16[1,384,1024]{1,0,2:T(2,128)(2,1)} copy(bf16[1,384,1024]{2,1,0:T(8,128)(2,1)} %fusion.7) | data formatting | bytes 1572864
  179.7 2.5 copy.48
  182.3 3.8 %convert_select_fusion.1 = bf16[1024,1024]{1,0:T(8,128)(2,1)} fusion(pred[1024]{0:T(1024)(128)(4,1)S(1)} %lt.50, bf16[1024,384]{0,1:T(8,128)(2,1)} %get-tuple-element.26, bf16[1,384,1024]{2,1,0:T(8,128)(2,1)S(1)} %all_gather.7), kind=kOutput, calls=%fused_computation.10 | convolution fusion | flops 807403520 | bytes 3671040 | tf_op jit(solution)/shard_map/dot_general | solution.py:13
  186.0 36.4 %all-to-all-done.4 = bf16[64,16,1024]{2,1,0:T(8,128)(2,1)S(1)} async-done(((bf16[64,16,1024]{2,1,0:T(8,128)(2,1)}), bf16[64,16,1024]{2,1,0:T(8,128)(2,1)S(1)}, u32[]{:S(2)}, u32[]{:S(2)}) %all-to-all-start.4) | async-done | bytes 2097184 | tf_op jit(solution)/shard_map/all_to_all | solution.py:112
  222.4 5.8 %all-to-all-start.2 = ((bf16[64,16,1024]{2,1,0:T(8,128)(2,1)}), bf16[64,16,1024]{2,1,0:T(8,128)(2,1)}, u32[]{:S(2)}, u32[]{:S(2)}) async-start(bf16[64,16,1024]{2,1,0:T(8,128)(2,1)} %bitcast.59), calls=%async_computation.2 | async-start | bytes 4194304 | tf_op jit(solution)/shard_map/all_to_all | solution.py:109
  228.5 4.8 %fusion.6 = bf16[1,1024,768]{2,1,0:T(8,128)(2,1)} fusion(bf16[1024,1024]{1,0:T(8,128)(2,1)} %bitcast.5, bf16[1024,384]{0,1:T(8,128)(2,1)} %copy-done.9, bf16[1024,384]{0,1:T(8,128)(2,1)S(1)} %copy-done.8), kind=kOutput, calls=%fused_computation.25 | convolution fusion | flops 1614544896 | bytes 5242880 | tf_op jit(solution)/shard_map/dot_general | solution.py:39
  236.3 38.8 %reduce-scatter.5.cloned.1.call-done = bf16[1,128,768]{2,1,0:T(8,128)(2,1)} async-done(((bf16[1,1024,768]{2,1,0:T(8,128)(2,1)}), bf16[1,128,768]{2,1,0:T(8,128)(2,1)}) %reduce-scatter.5.cloned.1.call-update) | async-done | bytes 196624 | tf_op jit(solution)/shard_map/reduce_scatter | solution.py:114
  276.8 2.8 gather_fusion.4
  281.9 4.6 %gather_fusion.1 = bf16[512,1024]{1,0:T(8,128)(2,1)S(1)} fusion(bf16[1024,1024]{1,0:T(8,128)(2,1)} %bitcast.9, s32[1024]{0:T(1024)S(1)} %pad_clamp_fusion), kind=kCustom, calls=%fused_computation.1 | custom fusion | bytes 2099200 | tf_op jit(solution)/shard_map/gather | solution.py:121
  287.2 3.7 %multiply_reduce_fusion = (f32[128,4]{1,0:T(8,128)S(1)}, bf16[128,1024]{1,0:T(8,128)(2,1)}) fusion(f32[128,4,1024]{2,1,0:T(4,128)S(1)} %reshape.206, f32[128,1024]{1,0:T(8,128)} %convert_element_type.75, f32[128,4]{1,0:T(8,128)S(1)} %copy.34), kind=kLoop, calls=%fused_computation.7 | loop fusion | flops 1965568 | bytes 2887680 | tf_op jit(solution)/shard_map/reduce_sum | solution.py:123
  (70 shorter events, 22.8 us)
Async XLA Ops:
  7.2 14.8 %copy-start = (bf16[128,1024]{1,0:T(8,128)(2,1)S(1)}, bf16[128,1024]{1,0:T(8,128)(2,1)}, u32[]{:S(2)}) copy-start(bf16[128,1024]{1,0:T(8,128)(2,1)} %param.6) | copy-start | bytes 786436
  10.6 19.2 %all-to-all-start = ((s32[64,1,1]{2,1,0:T(1,128)}), s32[64,1,1]{2,1,0:T(1,128)S(1)}, u32[]{:S(2)}, u32[]{:S(2)}) async-start(s32[64,1,1]{2,1,0:T(1,128)} %copy.36), calls=%async_computation | async-start | bytes 65536 | tf_op jit(solution)/shard_map/all_to_all | solution.py:105
  27.7 10.6 %copy-start.5 = (f32[128,4]{0,1:T(4,128)S(1)}, f32[128,4]{0,1:T(4,128)}, u32[]{:S(2)}) copy-start(f32[128,4]{0,1:T(4,128)} %param.8) | copy-start | bytes 6148
  29.8 59.6 %all-to-all-start.1 = ((bf16[64,16,1024]{2,1,0:T(8,128)(2,1)}), bf16[64,16,1024]{2,1,0:T(8,128)(2,1)}, u32[]{:S(2)}, u32[]{:S(2)}) async-start(bf16[64,16,1024]{2,1,0:T(8,128)(2,1)} %broadcast_select_fusion), calls=%async_computation.1 | async-start | bytes 4194304 | tf_op jit(solution)/shard_map/all_to_all | solution.py:104
  38.5 7.0 %copy-start.1 = (bf16[128,1024]{1,0:T(8,128)(2,1)S(1)}, bf16[128,1024]{1,0:T(8,128)(2,1)}, u32[]{:S(2)}) copy-start(bf16[128,1024]{1,0:T(8,128)(2,1)} %param.11) | copy-start | bytes 786436
  89.4 63.0 %all-to-all-start.3 = ((bf16[64,16,1024]{2,1,0:T(8,128)(2,1)}), bf16[64,16,1024]{2,1,0:T(8,128)(2,1)S(1)}, u32[]{:S(2)}, u32[]{:S(2)}) async-start(bf16[64,16,1024]{2,1,0:T(8,128)(2,1)} %fusion), calls=%async_computation.3 | async-start | bytes 4194304 | tf_op jit(solution)/shard_map/all_to_all | solution.py:110
  94.9 52.0 %all-gather.2.cloned.1.call-start = ((), (), s32[]{:S(2)}) async-start(), calls=%async_computation.7 | async-start | bytes 1769472 | tf_op jit(solution)/shard_map/all_gather | solution.py:98
  152.5 5.1 %copy-start.3 = (bf16[64,16,1024]{2,1,0:T(8,128)(2,1)}, bf16[64,16,1024]{2,1,0:T(8,128)(2,1)S(1)}, u32[]{:S(2)}) copy-start(bf16[64,16,1024]{2,1,0:T(8,128)(2,1)S(1)} %all-to-all-done.3) | copy-start | bytes 6291460
  152.5 5.1 %copy-start.6 = (bf16[1,1024,768]{2,1,0:T(8,128)(2,1)S(1)}, bf16[1,1024,768]{2,1,0:T(8,128)(2,1)}, u32[]{:S(2)}) copy-start(bf16[1,1024,768]{2,1,0:T(8,128)(2,1)} %all-gather.2.cloned.1.call-done) | copy-start | bytes 4718596
  157.6 3.3 %copy-start.7 = (bf16[1024,384]{0,1:T(8,128)(2,1)}, bf16[1024,384]{0,1:T(8,128)(2,1)S(1)}, u32[]{:S(2)}) copy-start(bf16[1024,384]{0,1:T(8,128)(2,1)S(1)} %get-tuple-element.24) | copy-start | bytes 2359300
  157.6 3.3 %copy-start.9 = (bf16[1024,384]{0,1:T(8,128)(2,1)}, bf16[1024,384]{0,1:T(8,128)(2,1)S(1)}, u32[]{:S(2)}) copy-start(bf16[1024,384]{0,1:T(8,128)(2,1)S(1)} %get-tuple-element.25) | copy-start | bytes 2359300
  160.9 61.5 %all-to-all-start.4 = ((bf16[64,16,1024]{2,1,0:T(8,128)(2,1)}), bf16[64,16,1024]{2,1,0:T(8,128)(2,1)S(1)}, u32[]{:S(2)}, u32[]{:S(2)}) async-start(bf16[64,16,1024]{2,1,0:T(8,128)(2,1)} %bitcast.62), calls=%async_computation.4 | async-start | bytes 4194304 | tf_op jit(solution)/shard_map/all_to_all | solution.py:112
  171.2 63.3 %reduce-scatter.7.cloned.1.call-start = ((), (), s32[]{:S(2)}) async-start(), calls=%async_computation.9 | async-start | bytes 884736
  222.4 6.0 %copy-start.8 = (bf16[1024,384]{0,1:T(8,128)(2,1)S(1)}, bf16[1024,384]{0,1:T(8,128)(2,1)}, u32[]{:S(2)}) copy-start(bf16[1024,384]{0,1:T(8,128)(2,1)} %copy-done.7) | copy-start | bytes 2359300
  222.4 59.4 %all-to-all-start.2 = ((bf16[64,16,1024]{2,1,0:T(8,128)(2,1)}), bf16[64,16,1024]{2,1,0:T(8,128)(2,1)}, u32[]{:S(2)}, u32[]{:S(2)}) async-start(bf16[64,16,1024]{2,1,0:T(8,128)(2,1)} %bitcast.59), calls=%async_computation.2 | async-start | bytes 4194304 | tf_op jit(solution)/shard_map/all_to_all | solution.py:109
  228.2 46.9 %reduce-scatter.5.cloned.1.call-start = ((), (), s32[]{:S(2)}) async-start(), calls=%async_computation.8 | async-start | bytes 1769472 | tf_op jit(solution)/shard_map/reduce_scatter | solution.py:114
  233.3 0.9 copy-start.4
  287.2 4.4 %copy-start.2 = (bf16[128,4,1024]{2,1,0:T(4,128)(2,1)S(1)}, bf16[128,4,1024]{2,1,0:T(4,128)(2,1)}, u32[]{:S(2)}) copy-start(bf16[128,4,1024]{2,1,0:T(4,128)(2,1)} %reshape.205) | copy-start | bytes 3145732
Sparse Core Ops, SparseCore 0:
  97.8 49.0 all-gather.1
  182.4 39.1 reduce-scatter.6
  233.4 41.6 reduce-scatter.4
where the time goes:
time: 301 us; the launch traced here: 300 us
  waiting for transfers between devices  131 us (44%)
  starting transfers between devices  40.9 us (14%)
  local copies, waits for them, and re-layouts  37.2 us (12%)
  blocking collectives  34.6 us (11%)
  matrix products  26.3 us (9%)
  other arithmetic  15.8 us (5%)
  between operations  14 us (5%)
    reduce_scatter x1, waiting for transfers between devices, local(): lax.psum_scatter(in_grad[None].astype(jnp.bfloat16), 'dp', scatter_dimens...  38.8 us
    all_to_all x1, waiting for transfers between devices, local(): lax.all_to_all(send_tokens, 'expert', split_axis=0, concat_axis=0, tiled=...  38.1 us
    all_to_all x1, waiting for transfers between devices, local(): lax.all_to_all(grad_back, 'expert', split_axis=0, concat_axis=0, tiled=True)  36.4 us
    all_gather x1, blocking collectives, local(): lax.all_gather(down_proj, 'dp', axis=2, tiled=True)  34.6 us
    all_gather x1, waiting for transfers between devices, local(): lax.all_gather(gate_up, 'dp', axis=1, tiled=True)  15.3 us
    all_to_all x1, starting transfers between devices, local(): lax.all_to_all(counts, 'expert', split_axis=0, concat_axis=0, tiled=True)  10.7 us
    all_to_all x1, starting transfers between devices, local(): lax.all_to_all(grad_back, 'expert', split_axis=0, concat_axis=0, tiled=True)  10.3 us
    unnamed x27, local copies, waits for them, and re-layouts  10.1 us
  transfers between devices with their start and end apart: 8, of which 5 were waited for; matrix products, arithmetic and copies ran while one was open for 19% of the time, Pallas kernels for 0%

commit v1 on v0

--- a/solution.py
+++ b/solution.py
@@ -2,6 +2,7 @@
 import jax.numpy as jnp
 from jax import lax
 from jax.sharding import PartitionSpec as P
+from jax.lax import all_to_all, axis_size
 
 
 def forward_rows(rows_in, weight_in, weight_out):
@@ -94,8 +95,15 @@
     send_grads = (slot_probs[:, None] * cotangent[token_of_slot].astype(jnp.float32)).astype(
         jnp.bfloat16
     )
+
+    def note_skins_up(u, mesh_name="dp"):
+        f_now = jnp.stack([u for _ in range(axis_size(mesh_name))])
+        n_now = all_to_all(f_now, mesh_name, 0, 0)
+        t_next = jnp.concatenate(n_now, axis=1)
+        return t_next
+
     weight_in, weight_out = (
-        lax.all_gather(gate_up, "dp", axis=1, tiled=True),
+        note_skins_up(gate_up),
         lax.all_gather(down_proj, "dp", axis=2, tiled=True),
     )
     weight_in = weight_in[0]

time: 301 us -> 340 us (1.13)
  the two profiles are of different devices: /device:TPU:2 before, /device:TPU:4 now
where the time goes in v1:
time: 340 us; the launch traced here: 339 us
  waiting for transfers between devices  165 us (49%)
  blocking collectives  43.1 us (13%)
  local copies, waits for them, and re-layouts  38.7 us (11%)
  starting transfers between devices  34.4 us (10%)
  matrix products  28.2 us (8%)
  other arithmetic  15.8 us (5%)
  between operations  14.3 us (4%)
    all_to_all x1, waiting for transfers between devices, local(): lax.all_to_all(send_tokens, 'expert', split_axis=0, concat_axis=0, tiled=...  38.2 us
    reduce_scatter x1, waiting for transfers between devices, local(): lax.psum_scatter(in_grad[None].astype(jnp.bfloat16), 'dp', scatter_dimens...  37.1 us
    all_to_all x1, waiting for transfers between devices, local(): lax.all_to_all(grad_back, 'expert', split_axis=0, concat_axis=0, tiled=True)  36.4 us
    all_to_all x1, waiting for transfers between devices, note_skins_up(): n_now = all_to_all(f_now, mesh_name, 0, 0)  33.7 us
    all_gather x1, blocking collectives, local(): lax.all_gather(down_proj, 'dp', axis=2, tiled=True)  24.9 us
    all_to_all x1, waiting for transfers between devices, local(): lax.all_to_all(send_grads, 'expert', split_axis=0, concat_axis=0, tiled=T...  19.4 us
    all_to_all x1, blocking collectives, local(): lax.all_to_all(counts, 'expert', split_axis=0, concat_axis=0, tiled=True)  18.2 us
    all_to_all x1, starting transfers between devices, note_skins_up(): n_now = all_to_all(f_now, mesh_name, 0, 0)  10.3 us
  transfers between devices with their start and end apart: 7, of which 5 were waited for; matrix products, arithmetic and copies ran while one was open for 16% of the time, Pallas kernels for 0%

profile of v1, /device:TPU:4, one launch (start us, length us, event | category | flops | bytes accessed | tf_op | source)
XLA Modules:
  0.0 339.4 jit_solution(7914620953448433860)
XLA Ops:
  10.0 18.2 %all_to_all.56 = s32[64,1,1]{2,1,0:T(1,128)S(1)} all-to-all(s32[64,1,1]{2,1,0:T(1,128)S(1)} %copy.36), channel_id=1, replica_groups=mesh['dp'=8,'expert'=64] {'expert'}, dimensions={0} | all-to-all | bytes 512 | tf_op jit(solution)/shard_map/all_to_all | solution.py:113
  30.4 10.3 %all-to-all-start.2 = ((bf16[8,1,128,768]{3,2,1,0:T(8,128)(2,1)}), bf16[8,1,128,768]{3,2,1,0:T(8,128)(2,1)}, u32[]{:S(2)}, u32[]{:S(2)}) async-start(bf16[8,1,128,768]{3,2,1,0:T(8,128)(2,1)} %stack.2), calls=%async_computation.2 | async-start | bytes 3145728 | tf_op jit(solution)/shard_map/all_to_all | solution.py:101
  41.4 4.1 %gather_fusion = bf16[1024,1024]{1,0:T(8,128)(2,1)S(1)} fusion(bf16[128,1024]{1,0:T(8,128)(2,1)S(1)} %copy-done, s32[1024]{0:T(1024)S(1)} %broadcast_clamp_fusion.1), kind=kCustom, calls=%fused_computation | custom fusion | bytes 4198400 | tf_op jit(solution)/shard_map/gather | solution.py:93
  47.1 33.7 %all-to-all-done.2 = bf16[8,1,128,768]{3,2,1,0:T(8,128)(2,1)} async-done(((bf16[8,1,128,768]{3,2,1,0:T(8,128)(2,1)}), bf16[8,1,128,768]{3,2,1,0:T(8,128)(2,1)}, u32[]{:S(2)}, u32[]{:S(2)}) %all-to-all-start.2) | async-done | bytes 1572896 | tf_op jit(solution)/shard_map/all_to_all | solution.py:101
  80.8 7.2 %all-to-all-start.1 = ((bf16[64,16,1024]{2,1,0:T(8,128)(2,1)}), bf16[64,16,1024]{2,1,0:T(8,128)(2,1)}, u32[]{:S(2)}, u32[]{:S(2)}) async-start(bf16[64,16,1024]{2,1,0:T(8,128)(2,1)} %broadcast_select_fusion), calls=%async_computation.1 | async-start | bytes 4194304 | tf_op jit(solution)/shard_map/all_to_all | solution.py:112
  88.3 6.9 %gather_fusion.2 = f32[1024]{0:T(1024)S(1)} fusion(f32[512]{0:T(512)S(1)} %reshape.207, s32[1024]{0:T(1024)S(1)} %broadcast_clamp_fusion), kind=kCustom, calls=%fused_computation.2 | custom fusion | bytes 12288 | tf_op jit(solution)/shard_map/gather | solution.py:94
  95.2 4.1 %gather_fusion.3 = bf16[1024,1024]{1,0:T(8,128)(2,1)S(1)} fusion(bf16[128,1024]{1,0:T(8,128)(2,1)S(1)} %copy-done.1, s32[1024]{0:T(1024)S(1)} %broadcast_clamp_fusion.1), kind=kCustom, calls=%fused_computation.3 | custom fusion | bytes 4198400 | tf_op jit(solution)/shard_map/gather | solution.py:95
  101.1 38.2 %all-to-all-done.1 = bf16[64,16,1024]{2,1,0:T(8,128)(2,1)} async-done(((bf16[64,16,1024]{2,1,0:T(8,128)(2,1)}), bf16[64,16,1024]{2,1,0:T(8,128)(2,1)}, u32[]{:S(2)}, u32[]{:S(2)}) %all-to-all-start.1) | async-done | bytes 2097184 | tf_op jit(solution)/shard_map/all_to_all | solution.py:112
  139.3 5.4 %all-to-all-start.4 = ((bf16[64,16,1024]{2,1,0:T(8,128)(2,1)}), bf16[64,16,1024]{2,1,0:T(8,128)(2,1)S(1)}, u32[]{:S(2)}, u32[]{:S(2)}) async-start(bf16[64,16,1024]{2,1,0:T(8,128)(2,1)} %fusion), calls=%async_computation.4 | async-start | bytes 4194304 | tf_op jit(solution)/shard_map/all_to_all | solution.py:118
  144.7 24.9 %all_gather.3 = bf16[1,384,1024]{2,1,0:T(8,128)(2,1)S(1)} all-gather(bf16[1,384,128]{2,1,0:T(8,128)(2,1)} %param.10), channel_id=1, replica_groups=mesh['dp'=8,'expert'=64] {'dp'}, dimensions={2}, use_global_device_ids=true | all-gather | bytes 884736 | tf_op jit(solution)/shard_map/all_gather | solution.py:107
  171.0 5.6 %fusion.13 = f32[1024,768]{0,1:T(8,128)} fusion(bf16[1024,1024]{1,0:T(8,128)(2,1)} %bitcast.5, bf16[1024,768]{1,0:T(8,128)(2,1)} %bitcast.7), kind=kOutput, calls=%fused_computation.56 | convolution fusion | flops 1610612736 | bytes 6815744 | tf_op jit(solution)/shard_map/dot_general | solution.py:10
  176.5 19.4 %all-to-all-done.4 = bf16[64,16,1024]{2,1,0:T(8,128)(2,1)S(1)} async-done(((bf16[64,16,1024]{2,1,0:T(8,128)(2,1)}), bf16[64,16,1024]{2,1,0:T(8,128)(2,1)S(1)}, u32[]{:S(2)}, u32[]{:S(2)}) %all-to-all-start.4) | async-done | bytes 2097184 | tf_op jit(solution)/shard_map/all_to_all | solution.py:118
  195.9 5.0 %multiply_convert_fusion.1 = (bf16[1024,384]{0,1:T(8,128)(2,1)S(1)}, bf16[1024,384]{0,1:T(8,128)(2,1)S(1)}, bf16[1024,384]{0,1:T(8,128)(2,1)}) fusion(f32[1024,768]{0,1:T(8,128)} %fusion.13, bf16[1024,1024]{1,0:T(8,128)(2,1)S(1)} %bitcast.59, bf16[1,384,1024]{2,1,0:T(8,128)(2,1)S(1)} %all_gather.3), kind=kOutput, calls=%fused_computation.18 | convolution fusion | flops 811204608 | bytes 8388608 | tf_op jit(solution)/shard_map/dot_general | solution.py:24
  201.0 5.3 %convert_select_fusion = bf16[1024,1024]{1,0:T(8,128)(2,1)} fusion(pred[1024]{0:T(1024)(128)(4,1)S(1)} %lt.50, bf16[1024,768]{1,0:T(8,128)(2,1)} %bitcast.7, bf16[1024,384]{0,1:T(8,128)(2,1)S(1)} %get-tuple-element.25, bf16[1024,384]{0,1:T(8,128)(2,1)S(1)} %get-tuple-element.24), kind=kOutput, calls=%fused_computation.8 | convolution fusion | flops 1615855616 | bytes 5243904 | tf_op jit(solution)/shard_map/dot_general | solution.py:37
  206.3 5.4 %all-to-all-start.5 = ((bf16[64,16,1024]{2,1,0:T(8,128)(2,1)}), bf16[64,16,1024]{2,1,0:T(8,128)(2,1)S(1)}, u32[]{:S(2)}, u32[]{:S(2)}) async-start(bf16[64,16,1024]{2,1,0:T(8,128)(2,1)} %bitcast.61), calls=%async_computation.5 | async-start | bytes 4194304 | tf_op jit(solution)/shard_map/all_to_all | solution.py:120
  211.8 3.7 %fusion.4 = bf16[1,384,1024]{2,1,0:T(8,128)(2,1)} fusion(bf16[1024,384]{0,1:T(8,128)(2,1)} %get-tuple-element.26, bf16[1024,1024]{1,0:T(8,128)(2,1)} %bitcast.60), kind=kOutput, calls=%fused_computation.24 | convolution fusion | flops 805699584 | bytes 3670016 | tf_op jit(solution)/shard_map/dot_general | solution.py:43
  215.5 4.8 %copy.42 = bf16[1,384,1024]{1,0,2:T(2,128)(2,1)} copy(bf16[1,384,1024]{2,1,0:T(8,128)(2,1)} %fusion.4) | data formatting | bytes 1572864
  222.8 3.8 %convert_select_fusion.1 = bf16[1024,1024]{1,0:T(8,128)(2,1)} fusion(pred[1024]{0:T(1024)(128)(4,1)S(1)} %lt.50, bf16[1024,384]{0,1:T(8,128)(2,1)} %get-tuple-element.26, bf16[1,384,1024]{2,1,0:T(8,128)(2,1)S(1)} %all_gather.3), kind=kOutput, calls=%fused_computation.10 | convolution fusion | flops 807403520 | bytes 3671040 | tf_op jit(solution)/shard_map/dot_general | solution.py:14
  226.6 36.4 %all-to-all-done.5 = bf16[64,16,1024]{2,1,0:T(8,128)(2,1)S(1)} async-done(((bf16[64,16,1024]{2,1,0:T(8,128)(2,1)}), bf16[64,16,1024]{2,1,0:T(8,128)(2,1)S(1)}, u32[]{:S(2)}, u32[]{:S(2)}) %all-to-all-start.5) | async-done | bytes 2097184 | tf_op jit(solution)/shard_map/all_to_all | solution.py:120
  263.0 5.7 %all-to-all-start.3 = ((bf16[64,16,1024]{2,1,0:T(8,128)(2,1)}), bf16[64,16,1024]{2,1,0:T(8,128)(2,1)}, u32[]{:S(2)}, u32[]{:S(2)}) async-start(bf16[64,16,1024]{2,1,0:T(8,128)(2,1)} %bitcast.58), calls=%async_computation.3 | async-start | bytes 4194304 | tf_op jit(solution)/shard_map/all_to_all | solution.py:117
  269.0 4.8 %fusion.3 = bf16[1,1024,768]{2,1,0:T(8,128)(2,1)} fusion(bf16[1024,1024]{1,0:T(8,128)(2,1)} %bitcast.5, bf16[1024,384]{0,1:T(8,128)(2,1)} %copy-done.8, bf16[1024,384]{0,1:T(8,128)(2,1)S(1)} %copy-done.7), kind=kOutput, calls=%fused_computation.22 | convolution fusion | flops 1614544896 | bytes 5242880 | tf_op jit(solution)/shard_map/dot_general | solution.py:40
  276.9 37.1 %reduce-scatter.5.cloned.1.call-done = bf16[1,128,768]{2,1,0:T(8,128)(2,1)} async-done(((bf16[1,1024,768]{2,1,0:T(8,128)(2,1)}), bf16[1,128,768]{2,1,0:T(8,128)(2,1)}) %reduce-scatter.5.cloned.1.call-update) | async-done | bytes 196624 | tf_op jit(solution)/shard_map/reduce_scatter | solution.py:122
  320.7 4.6 %gather_fusion.1 = bf16[512,1024]{1,0:T(8,128)(2,1)S(1)} fusion(bf16[1024,1024]{1,0:T(8,128)(2,1)} %bitcast.10, s32[1024]{0:T(1024)S(1)} %pad_clamp_fusion), kind=kCustom, calls=%fused_computation.1 | custom fusion | bytes 2099200 | tf_op jit(solution)/shard_map/gather | solution.py:129
  326.1 3.7 %multiply_reduce_fusion = (f32[128,4]{1,0:T(8,128)S(1)}, bf16[128,1024]{1,0:T(8,128)(2,1)}) fusion(f32[128,4,1024]{2,1,0:T(4,128)S(1)} %reshape.209, f32[128,1024]{1,0:T(8,128)} %convert_element_type.75, f32[128,4]{1,0:T(8,128)S(1)} %copy.34), kind=kLoop, calls=%fused_computation.7 | loop fusion | flops 1965568 | bytes 2887680 | tf_op jit(solution)/shard_map/reduce_sum | solution.py:131
  (67 shorter events, 26.8 us)
Async XLA Ops:
  7.2 34.3 %copy-start = (bf16[128,1024]{1,0:T(8,128)(2,1)S(1)}, bf16[128,1024]{1,0:T(8,128)(2,1)}, u32[]{:S(2)}) copy-start(bf16[128,1024]{1,0:T(8,128)(2,1)} %param.6) | copy-start | bytes 786436
  30.4 50.4 %all-to-all-start.2 = ((bf16[8,1,128,768]{3,2,1,0:T(8,128)(2,1)}), bf16[8,1,128,768]{3,2,1,0:T(8,128)(2,1)}, u32[]{:S(2)}, u32[]{:S(2)}) async-start(bf16[8,1,128,768]{3,2,1,0:T(8,128)(2,1)} %stack.2), calls=%async_computation.2 | async-start | bytes 3145728 | tf_op jit(solution)/shard_map/all_to_all | solution.py:101
  47.1 40.9 %copy-start.5 = (f32[128,4]{0,1:T(4,128)S(1)}, f32[128,4]{0,1:T(4,128)}, u32[]{:S(2)}) copy-start(f32[128,4]{0,1:T(4,128)} %param.8) | copy-start | bytes 6148
  80.8 58.5 %all-to-all-start.1 = ((bf16[64,16,1024]{2,1,0:T(8,128)(2,1)}), bf16[64,16,1024]{2,1,0:T(8,128)(2,1)}, u32[]{:S(2)}, u32[]{:S(2)}) async-start(bf16[64,16,1024]{2,1,0:T(8,128)(2,1)} %broadcast_select_fusion), calls=%async_computation.1 | async-start | bytes 4194304 | tf_op jit(solution)/shard_map/all_to_all | solution.py:112
  88.3 7.0 %copy-start.1 = (bf16[128,1024]{1,0:T(8,128)(2,1)S(1)}, bf16[128,1024]{1,0:T(8,128)(2,1)}, u32[]{:S(2)}) copy-start(bf16[128,1024]{1,0:T(8,128)(2,1)} %param.11) | copy-start | bytes 786436
  139.3 56.7 %all-to-all-start.4 = ((bf16[64,16,1024]{2,1,0:T(8,128)(2,1)}), bf16[64,16,1024]{2,1,0:T(8,128)(2,1)S(1)}, u32[]{:S(2)}, u32[]{:S(2)}) async-start(bf16[64,16,1024]{2,1,0:T(8,128)(2,1)} %fusion), calls=%async_computation.4 | async-start | bytes 4194304 | tf_op jit(solution)/shard_map/all_to_all | solution.py:118
  195.9 5.0 %copy-start.3 = (bf16[64,16,1024]{2,1,0:T(8,128)(2,1)}, bf16[64,16,1024]{2,1,0:T(8,128)(2,1)S(1)}, u32[]{:S(2)}) copy-start(bf16[64,16,1024]{2,1,0:T(8,128)(2,1)S(1)} %all-to-all-done.4) | copy-start | bytes 6291460
  201.0 5.3 %copy-start.6 = (bf16[1024,384]{0,1:T(8,128)(2,1)}, bf16[1024,384]{0,1:T(8,128)(2,1)S(1)}, u32[]{:S(2)}) copy-start(bf16[1024,384]{0,1:T(8,128)(2,1)S(1)} %get-tuple-element.24) | copy-start | bytes 2359300
  201.0 5.3 %copy-start.8 = (bf16[1024,384]{0,1:T(8,128)(2,1)}, bf16[1024,384]{0,1:T(8,128)(2,1)S(1)}, u32[]{:S(2)}) copy-start(bf16[1024,384]{0,1:T(8,128)(2,1)S(1)} %get-tuple-element.25) | copy-start | bytes 2359300
  206.3 56.7 %all-to-all-start.5 = ((bf16[64,16,1024]{2,1,0:T(8,128)(2,1)}), bf16[64,16,1024]{2,1,0:T(8,128)(2,1)S(1)}, u32[]{:S(2)}, u32[]{:S(2)}) async-start(bf16[64,16,1024]{2,1,0:T(8,128)(2,1)} %bitcast.61), calls=%async_computation.5 | async-start | bytes 4194304 | tf_op jit(solution)/shard_map/all_to_all | solution.py:120
  211.7 63.3 %reduce-scatter.7.cloned.1.call-start = ((), (), s32[]{:S(2)}) async-start(), calls=%async_computation.9 | async-start | bytes 884736
  263.0 6.0 %copy-start.7 = (bf16[1024,384]{0,1:T(8,128)(2,1)S(1)}, bf16[1024,384]{0,1:T(8,128)(2,1)}, u32[]{:S(2)}) copy-start(bf16[1024,384]{0,1:T(8,128)(2,1)} %copy-done.6) | copy-start | bytes 2359300
  263.0 57.8 %all-to-all-start.3 = ((bf16[64,16,1024]{2,1,0:T(8,128)(2,1)}), bf16[64,16,1024]{2,1,0:T(8,128)(2,1)}, u32[]{:S(2)}, u32[]{:S(2)}) async-start(bf16[64,16,1024]{2,1,0:T(8,128)(2,1)} %bitcast.58), calls=%async_computation.3 | async-start | bytes 4194304 | tf_op jit(solution)/shard_map/all_to_all | solution.py:117
  268.7 45.3 %reduce-scatter.5.cloned.1.call-start = ((), (), s32[]{:S(2)}) async-start(), calls=%async_computation.8 | async-start | bytes 1769472 | tf_op jit(solution)/shard_map/reduce_scatter | solution.py:122
  273.9 0.9 copy-start.4
  326.1 4.4 %copy-start.2 = (bf16[128,4,1024]{2,1,0:T(4,128)(2,1)S(1)}, bf16[128,4,1024]{2,1,0:T(4,128)(2,1)}, u32[]{:S(2)}) copy-start(bf16[128,4,1024]{2,1,0:T(4,128)(2,1)} %reshape.208) | copy-start | bytes 3145732
Sparse Core Ops, SparseCore 0:
  222.9 37.5 reduce-scatter.6
  274.0 39.9 reduce-scatter.4
